TPU v7x, 32 devices: a whole 2x2x4 slice. The times are simulated.
32 devices in a mesh: dp: 16 (over z, y, x), mp: 2 (over core).
Axes of the slice: x: 2, y: 2, z: 4, core: 2. Of those that a mesh axis runs over, the one named last changes fastest.
Arguments:
- tokens: bfloat16 [7168, 4544], P('dp'), may hold values from -32 to 32
- layer_norm_gain: bfloat16 [4544], replicated, may hold values from 0.5 to 1.5
- layer_norm_bias: bfloat16 [4544], replicated, may hold values from -3 to 3
- query_weight: bfloat16 [4544, 4096], P('dp', 'mp'), may hold values from -3 to 3
- key_value_weight: bfloat16 [4544, 128], P('dp'), may hold values from -3 to 3
- output_weight: bfloat16 [4096, 4544], P('dp', 'mp'), may hold values from -0.09375 to 0.09375
- adapter_down_factors: bfloat16 [16, 4544, 16], P('dp', 'mp'), may hold values from -0.09375 to 0.09375
- adapter_up_factors: bfloat16 [16, 16, 4096], P('dp', None, 'mp'), may hold values from -1.5 to 1.5
- lengths: int32 [16, 4], P('dp'), may hold values from 1 to 224, 448 in all within a row
- prompt_adapter: int32 [16, 4], P('dp'), may hold values from 0 to 15
- prompt_page_table: int32 [16, 8], P('dp'), may hold values from 0 to 7, each once within a row
- adapter_storage: int32 [16], replicated, may hold values from 0 to 15, each once
Outputs:
- attn_proj: bfloat16 [7168, 4544], P('dp', 'mp')
- kv_cache: bfloat16 [128, 128, 128], P('dp')
Inputs may be any that keep to these rules, and one draw needn't show every extreme that they name: `lengths`: each row sums to 448. `prompt_page_table`: row r lists each of the 8 pages of the pool of dp index r once; entry p * 2 + k is the page of tokens k * 128 to (k + 1) * 128 - 1 of that row's prompt p. `adapter_storage`: every storage slot holds exactly one adapter.
All inputs are finite; a program needn't handle non-finite values.
Results may differ from a plain program's by a relative error of at most 0.012.
The roundings to bfloat16 on the way count: a program that leaves them out, or rounds other values in their place, can miss the bound.
Values may be sent and summed in bfloat16 or wider, within the bound.
No kernel may reach another device: no remote copies, remote signals or barrier semaphores. Data moves between devices by JAX's collectives and lax.ppermute only.
A program may use at most 192 MiB of HBM per device.

v0:
```python
import math

import jax
import jax.numpy as jnp
from jax import lax
from jax.sharding import PartitionSpec as P

HEAD_SIZE = 64
PAGE = 128


def layer_norm(tokens, layer_norm_gain, layer_norm_bias):
    values = tokens.astype(jnp.float32)
    row_mean = jnp.mean(values, axis=-1, keepdims=True)
    centred = values - row_mean
    row_var = jnp.mean(centred * centred, axis=-1, keepdims=True)
    scaled = centred * lax.rsqrt(row_var + 1e-05)
    return (
        scaled * layer_norm_gain.astype(jnp.float32) + layer_norm_bias.astype(jnp.float32)
    ).astype(jnp.bfloat16)


def layout(lengths_row, row_number_count):
    prompt_end = jnp.cumsum(lengths_row)
    prompt_start = prompt_end - lengths_row
    row_index = jnp.arange(row_number_count, dtype=jnp.int32)
    member = (row_index[:, None] >= prompt_start[None, :]) & (
        row_index[:, None] < prompt_end[None, :]
    )
    first_row = jnp.sum(jnp.where(member, prompt_start[None, :], 0), axis=1)
    prompt_numbers = jnp.arange(lengths_row.shape[0], dtype=jnp.int32)
    prompt_index = jnp.sum(jnp.where(member, prompt_numbers[None, :], 0), axis=1)
    position = (row_index - first_row).astype(jnp.float32)
    return (member, position, prompt_start, prompt_index)


def rotate(values, position):
    half_width = values.shape[-1] // 2
    frequency = jnp.exp(
        jnp.arange(half_width, dtype=jnp.float32) * (-math.log(10000.0) / half_width)
    )
    angles = position[:, None, None] * frequency[None, None, :]
    cosine = jnp.cos(angles)
    sine = jnp.sin(angles)
    leading = values[..., :half_width]
    trailing = values[..., half_width:]
    return jnp.concatenate(
        [leading * cosine - trailing * sine, trailing * cosine + leading * sine], axis=-1
    )


def attend(queries, keys_rot, values, prompt_index):
    row_number_count = queries.shape[0]
    head_width = queries.shape[2]
    row_index = jnp.arange(row_number_count, dtype=jnp.int32)
    allowed = (prompt_index[:, None] == prompt_index[None, :]) & (
        row_index[None, :] <= row_index[:, None]
    )
    scores = jnp.einsum("thd,sd->hts", queries, keys_rot, preferred_element_type=jnp.float32) * (
        1.0 / math.sqrt(head_width)
    )
    scores = jnp.where(allowed[None, :, :], scores, -jnp.inf)
    row_peak = jnp.max(scores, axis=-1, keepdims=True)
    weights = jnp.exp(scores - row_peak)
    probs = (weights / jnp.sum(weights, axis=-1, keepdims=True)).astype(jnp.bfloat16)
    context = jnp.einsum("hts,sd->thd", probs, values, preferred_element_type=jnp.float32)
    return context.astype(jnp.bfloat16)


def fill_pages(kv_rot, lengths_row, prompt_start, table_row, page_slots):
    page_count = table_row.shape[0]
    prompt_count = lengths_row.shape[0]
    per_prompt = page_count // prompt_count
    page_index = jnp.arange(page_count, dtype=jnp.int32)
    entry = jnp.sum(
        jnp.where(table_row[None, :] == page_index[:, None], page_index[None, :], 0), axis=1
    )
    prompt_of = entry // per_prompt
    page_of = entry % per_prompt
    prompt_numbers = jnp.arange(prompt_count, dtype=jnp.int32)
    chosen = prompt_of[:, None] == prompt_numbers[None, :]
    prompt_len = jnp.sum(jnp.where(chosen, lengths_row[None, :], 0), axis=1)
    base_row = jnp.sum(jnp.where(chosen, prompt_start[None, :], 0), axis=1)
    within = page_of[:, None] * page_slots + jnp.arange(page_slots, dtype=jnp.int32)[None, :]
    valid = within < prompt_len[:, None]
    source = jnp.minimum(base_row[:, None] + within, kv_rot.shape[0] - 1)
    return jnp.where(valid[:, :, None], kv_rot[source], jnp.zeros((), kv_rot.dtype))


def shards(
    tokens,
    layer_norm_gain,
    layer_norm_bias,
    query_weight,
    key_value_weight,
    output_weight,
    adapter_down_factors,
    adapter_up_factors,
    lengths,
    prompt_adapter,
    prompt_page_table,
    adapter_storage,
):
    row_number_count = tokens.shape[0]
    group_count = lengths.shape[0]
    group_rows = row_number_count // group_count
    prompt_count = lengths.shape[1]
    total_prompts = group_count * prompt_count
    member_grouped, position_grouped, start_grouped, index_grouped = jax.vmap(
        lambda one_row: layout(one_row, group_rows)
    )(lengths)
    position = position_grouped.reshape(row_number_count)
    prompt_global = (
        index_grouped + (jnp.arange(group_count, dtype=jnp.int32) * prompt_count)[:, None]
    ).reshape(row_number_count)
    member_weight = (
        prompt_global[:, None] == jnp.arange(total_prompts, dtype=jnp.int32)[None, :]
    ).astype(jnp.float32)
    normed = layer_norm(tokens, layer_norm_gain, layer_norm_bias)

    def add_rows(piece):
        return jnp.dot(normed, piece, preferred_element_type=jnp.float32)

    query_base = add_rows(lax.all_gather(query_weight, "dp", axis=0, tiled=True))
    kv_base = add_rows(lax.all_gather(key_value_weight, "dp", axis=0, tiled=True))
    adapters_flat = prompt_adapter.reshape(total_prompts)
    adapter_count = adapter_storage.shape[0]
    adapter_numbers = jnp.arange(adapter_count, dtype=jnp.int32)
    storage_slots = jnp.sum(
        jnp.where(adapter_numbers[None, :] == adapters_flat[:, None], adapter_storage[None, :], 0),
        axis=1,
    )
    pieces = (
        lax.all_gather(adapter_down_factors, "dp", axis=0, tiled=True),
        lax.all_gather(adapter_up_factors, "dp", axis=0, tiled=True),
    )
    piece_rows = pieces[0].shape[0]
    matches = (storage_slots[:, None] == jnp.arange(piece_rows, dtype=jnp.int32)[None, :]).astype(
        jnp.bfloat16
    )
    down_part = jnp.einsum("pn,ndr->pdr", matches, pieces[0], preferred_element_type=jnp.float32)
    up_part = jnp.einsum("pn,nrc->prc", matches, pieces[1], preferred_element_type=jnp.float32)
    down_selected = down_part.astype(jnp.bfloat16)
    up_selected = up_part.astype(jnp.bfloat16)
    feature_columns = adapter_down_factors.shape[1]
    features = lax.dynamic_slice_in_dim(
        normed, lax.axis_index("mp") * feature_columns, feature_columns, 1
    )
    rank_portion = jnp.zeros((row_number_count, adapter_down_factors.shape[2]), jnp.float32)
    for prompt in range(total_prompts):
        rank_portion = rank_portion + member_weight[:, prompt : prompt + 1] * jnp.dot(
            features, down_selected[prompt], preferred_element_type=jnp.float32
        )
    ranks = lax.psum(rank_portion, "mp").astype(jnp.bfloat16)
    adapted_queries = jnp.zeros((row_number_count, adapter_up_factors.shape[2]), jnp.float32)
    for prompt in range(total_prompts):
        adapted_queries = adapted_queries + member_weight[:, prompt : prompt + 1] * jnp.dot(
            ranks, up_selected[prompt], preferred_element_type=jnp.float32
        )
    queries = rotate(
        (query_base + adapted_queries).reshape(row_number_count, -1, HEAD_SIZE), position
    ).astype(jnp.bfloat16)
    keys_rot = rotate(kv_base[:, None, :HEAD_SIZE], position)[:, 0, :]
    kv_rot = jnp.concatenate([keys_rot, kv_base[:, HEAD_SIZE:]], axis=1).astype(jnp.bfloat16)
    local_heads = queries.shape[1]
    queries_grouped = queries.reshape(group_count, group_rows, local_heads, HEAD_SIZE)
    kv_grouped = kv_rot.reshape(group_count, group_rows, 2 * HEAD_SIZE)
    context_grouped = jax.vmap(
        lambda q_part, kv_part, idx_part: attend(
            q_part, kv_part[:, :HEAD_SIZE], kv_part[:, HEAD_SIZE:], idx_part
        )
    )(queries_grouped, kv_grouped, index_grouped)
    context = context_grouped.reshape(row_number_count, local_heads * HEAD_SIZE)
    context_all = lax.all_gather(context, "mp", axis=1, tiled=True)
    projected = jnp.dot(
        context_all,
        lax.all_gather(output_weight, "dp", axis=0, tiled=True),
        preferred_element_type=jnp.float32,
    )
    attn_proj = projected.astype(jnp.bfloat16)
    cache_grouped = jax.vmap(
        lambda kv_part, len_part, start_part, table_part: fill_pages(
            kv_part, len_part, start_part, table_part, PAGE
        )
    )(kv_grouped, lengths, start_grouped, prompt_page_table)
    kv_cache = cache_grouped.reshape(group_count * prompt_page_table.shape[1], PAGE, 2 * HEAD_SIZE)
    return (attn_proj, kv_cache)


def solution(mesh):
    return jax.shard_map(
        shards,
        mesh=mesh,
        in_specs=(
            P("dp", None),
            P(),
            P(),
            P("dp", "mp"),
            P("dp", None),
            P("dp", "mp"),
            P("dp", "mp", None),
            P("dp", None, "mp"),
            P("dp", None),
            P("dp", None),
            P("dp", None),
            P(),
        ),
        out_specs=(P("dp", "mp"), P("dp", None, None)),
        check_vma=False,
    )
```

profile of v0, /device:TPU:0, one launch (start us, length us, event | category | flops | bytes accessed | tf_op | source)
XLA Modules:
  0.0 819.4 jit_solution(24132339431085566)
XLA Ops:
  7.2 0.0 all-gather.11.cloned.1.call-start
  7.2 0.7 all-gather.11.cloned.1.call-update
  7.9 0.0 all-gather.17.cloned.1.call-start
  7.9 0.7 all-gather.17.cloned.1.call-update
  8.6 0.0 all-gather.9.cloned.1.call-start
  8.7 0.7 all-gather.9.cloned.1.call-update
  9.4 0.0 all-gather.19.cloned.1.call-start
  9.4 0.5 all-gather.19.cloned.1.call-update
  10.0 0.0 all-gather.15.cloned.1.call-start
  10.0 0.5 all-gather.15.cloned.1.call-update
  10.5 0.0 all-gather.13.cloned.1.call-start
  10.6 0.8 reduce_window_sum.11
  11.4 0.7 convert_element_type.61
  12.1 0.7 convert_element_type.62
  12.8 1.0 select_reduce_fusion.5
  13.9 0.9 subtract_bitcast_fusion
  14.8 0.1 select_reduce_fusion
  14.9 2.8 convert_reduce_fusion
  17.7 1.2 fusion.6
  18.9 0.3 multiply_cosine_fusion
  19.3 0.2 fusion.48
  19.5 4.2 fusion.9
  23.7 44.9 %all-gather.11.cloned.1.call-done = bf16[16,16,2048]{2,1,0:T(8,128)(2,1)} async-done(((bf16[1,16,2048]{2,1,0:T(8,128)(2,1)}), bf16[16,16,2048]{2,1,0:T(8,128)(2,1)}) %all-gather.11.cloned.1.call-update) | async-done | bytes 1048592 | tf_op jit(solution)/shard_map/all_gather | solution.py:135
  68.6 2.4 convolution_convert_fusion.2
  71.0 0.4 fusion.101
  71.4 54.8 %all-gather.17.cloned.1.call-done = bf16[16,284,128]{2,1,0:T(8,128)(2,1)} async-done(((bf16[1,284,128]{2,1,0:T(8,128)(2,1)}), bf16[16,284,128]{2,1,0:T(8,128)(2,1)}) %all-gather.17.cloned.1.call-update) | async-done | bytes 1163280 | tf_op jit(solution)/shard_map/all_gather | solution.py:125
  126.2 1.4 reshape.839
  127.5 56.1 %all-gather.9.cloned.1.call-done = bf16[16,2272,16]{1,2,0:T(8,128)(2,1)} async-done(((bf16[1,2272,16]{1,2,0:T(8,128)(2,1)}), bf16[16,2272,16]{1,2,0:T(8,128)(2,1)}) %all-gather.9.cloned.1.call-update) | async-done | bytes 1163280 | tf_op jit(solution)/shard_map/all_gather | solution.py:134
  183.6 1.9 convolution_convert_fusion.1
  185.6 0.4 fusion.100
  186.0 2.5 fusion.38
  188.5 0.0 copy-done
  188.5 0.9 fusion.41
  189.4 0.9 fusion.44
  190.3 0.9 fusion.35
  191.3 3.6 psum.7
  194.9 3.8 fusion.103
  198.7 0.3 fusion.62
  199.0 2.5 fusion.68
  201.5 2.5 fusion.71
  204.0 2.4 fusion.74
  206.4 2.5 fusion.65
  208.9 187.0 %all-gather.19.cloned.1.call-done = bf16[16,284,2048]{2,1,0:T(8,128)(2,1)} async-done(((bf16[1,284,2048]{2,1,0:T(8,128)(2,1)}), bf16[16,284,2048]{2,1,0:T(8,128)(2,1)}) %all-gather.19.cloned.1.call-update) | async-done | bytes 18612240 | tf_op jit(solution)/shard_map/all_gather | solution.py:124
  395.9 15.9 %reshape.841 = bf16[4544,2048]{1,0:T(8,128)(2,1)} reshape(bf16[16,284,2048]{2,1,0:T(8,128)(2,1)} %all-gather.19.cloned.1.call-done) | data formatting | bytes 37224448
  411.8 18.4 %add_add_fusion = f32[448,2048]{1,0:T(8,128)} fusion(f32[448,2048]{1,0:T(8,128)} %fusion.65, f32[448,2048]{1,0:T(8,128)} %fusion.68, f32[448,2048]{1,0:T(8,128)} %fusion.71, f32[448,2048]{1,0:T(8,128)} %fusion.74, bf16[448,4544]{1,0:T(8,128)(2,1)} %fusion.9, bf16[4544,2048]{1,0:T(8,128)(2,1)} %reshape.841, f32[448]{0:T(512)S(1)} %bitcast.104, ...), kind=kOutput, calls=%fused_computation.17 | convolution fusion | flops 8345616384 | bytes 41040896 | tf_op jit(solution)/shard_map/dot_general | solution.py:122
  430.2 5.2 copy.43
  435.4 3.0 subtract_convert_fusion
  438.4 12.0 %fusion.1 = (f32[32,448]{1,0:T(8,128)S(1)}, f32[448,448,32]{1,0,2:T(8,128)}) fusion(pred[448,448]{0,1:T(8,128)(4,1)S(1)} %fusion.48, bf16[448,32,32]{0,2,1:T(8,128)(2,1)S(1)} %get-tuple-element.7, bf16[448,32,32]{0,2,1:T(8,128)(2,1)S(1)} %get-tuple-element.6, bf16[448,1,32]{0,2,1:T(8,128)(2,1)S(1)} %get-tuple-element.17, ...), kind=kOutput, calls=%fused_computation.5 | convolution fusion | flops 845121536 | bytes 27840512 | tf_op jit(solution)/shard_map/vmap(thd,sd->hts)/dot_general | solution.py:59
  450.3 13.3 %fusion = f32[32,448]{1,0:T(8,128)S(1)} fusion(f32[448,448,32]{1,0,2:T(8,128)} %get-tuple-element.27, f32[32,448]{1,0:T(8,128)S(1)} %get-tuple-element.26, pred[448,448]{0,1:T(8,128)(4,1)S(1)} %fusion.48), kind=kLoop, calls=%fused_computation.4 | loop fusion | flops 25675776 | bytes 26005504 | tf_op jit(solution)/shard_map/vmap()/reduce_sum | solution.py:65
  463.6 0.0 copy-start.3
  463.6 0.0 copy-start.2
  463.7 14.3 %fusion.14 = bf16[64,32,448]{2,0,1:T(8,128)(2,1)} fusion(f32[32,448]{1,0:T(8,128)S(1)} %fusion, f32[32,448]{1,0:T(8,128)S(1)} %get-tuple-element.26, f32[448,448,32]{1,0,2:T(8,128)} %get-tuple-element.27, pred[448,448]{0,1:T(8,128)(4,1)S(1)} %fusion.48, f32[448,128]{0,1:T(8,128)S(1)} %fusion.103), kind=kOutput, calls=%fused_computation.26 | convolution fusion | flops 855113728 | bytes 27951104 | tf_op jit(solution)/shard_map/vmap(hts,sd->thd)/dot_general | solution.py:66
  478.0 0.0 all-gather.13.cloned.1.call-update
  478.0 0.1 select_reduce_fusion.2
  478.1 0.0 copy-done.2
  478.1 0.1 select_reduce_fusion.4
  478.2 0.1 compare_select_fusion
  478.3 0.1 add_compare_fusion
  478.4 0.1 copy.45
  478.6 4.7 gather_fusion
  483.3 0.9 broadcast_select_fusion
  484.2 294.9 %all-gather.15.cloned.1.call-done = bf16[4096,2272]{0,1:T(8,128)(2,1)} async-done(((bf16[256,2272]{0,1:T(8,128)(2,1)}), bf16[4096,2272]{0,1:T(8,128)(2,1)}) %all-gather.15.cloned.1.call-update) | async-done | bytes 18612240 | tf_op jit(solution)/shard_map/all_gather | solution.py:177
  779.1 16.3 %all-gather.13.cloned.1.call-done = bf16[448,4096]{0,1:T(8,128)(2,1)} async-done(((bf16[448,2048]{0,1:T(8,128)(2,1)}), bf16[448,4096]{0,1:T(8,128)(2,1)}) %all-gather.13.cloned.1.call-update) | async-done | bytes 3670032 | tf_op jit(solution)/shard_map/all_gather | solution.py:174
  795.4 17.2 %convolution_convert_fusion = bf16[448,2272]{1,0:T(8,128)(2,1)} fusion(bf16[448,4096]{0,1:T(8,128)(2,1)} %all-gather.13.cloned.1.call-done, bf16[4096,2272]{0,1:T(8,128)(2,1)} %all-gather.15.cloned.1.call-done), kind=kOutput, calls=%fused_computation.16 | convolution fusion | flops 8339294208 | bytes 24317952 | tf_op jit(solution)/shard_map/dot_general | solution.py:175
  (17 shorter events, 0.1 us)
Async XLA Ops:
  7.2 61.4 %all-gather.11.cloned.1.call-start = ((), (), s32[]{:S(2)}) async-start(), calls=%async_computation.1 | async-start | bytes 1114112 | tf_op jit(solution)/shard_map/all_gather | solution.py:135
  7.9 118.3 %all-gather.17.cloned.1.call-start = ((), (), s32[]{:S(2)}) async-start(), calls=%async_computation.4 | async-start | bytes 1253376 | tf_op jit(solution)/shard_map/all_gather | solution.py:125
  8.6 175.0 %all-gather.9.cloned.1.call-start = ((), (), s32[]{:S(2)}) async-start(), calls=%async_computation | async-start | bytes 1253376 | tf_op jit(solution)/shard_map/all_gather | solution.py:134
  9.4 386.5 %all-gather.19.cloned.1.call-start = ((), (), s32[]{:S(2)}) async-start(), calls=%async_computation.5 | async-start | bytes 20054016 | tf_op jit(solution)/shard_map/all_gather | solution.py:124
  10.0 769.2 %all-gather.15.cloned.1.call-start = ((), (), s32[]{:S(2)}) async-start(), calls=%async_computation.3 | async-start | bytes 19775488 | tf_op jit(solution)/shard_map/all_gather | solution.py:177
  10.5 784.9 %all-gather.13.cloned.1.call-start = ((), (), s32[]{:S(2)}) async-start(), calls=%async_computation.2 | async-start | bytes 6291456 | tf_op jit(solution)/shard_map/all_gather | solution.py:174
  12.8 4.8 copy-start.1
  183.6 4.9 copy-start
  463.6 14.3 %copy-start.3 = (s32[1,8]{1,0:T(1,128)S(1)}, s32[1,8]{1,0:T(1,128)}, u32[]{:S(2)}) copy-start(s32[1,8]{1,0:T(1,128)} %param.22) | copy-start | bytes 100
  463.6 14.5 %copy-start.2 = (s32[1,4]{1,0:T(1,128)S(1)}, s32[1,4]{1,0:T(1,128)}, u32[]{:S(2)}) copy-start(s32[1,4]{1,0:T(1,128)} %param.20) | copy-start | bytes 52
Sparse Core Ops, SparseCore 0:
  10.7 57.8 all-gather.10
  71.4 54.7 all-gather.16
  129.0 54.6 all-gather.8
  186.3 209.5 all-gather.18
  397.2 381.8 all-gather.14
  780.5 14.8 all-gather.12
where the time goes:
time: 820 us; the launch traced here: 819 us
  waiting for transfers between devices  657 us (80%)
  matrix products  85.1 us (10%)
  other arithmetic  30.9 us (4%)
  local copies, waits for them, and re-layouts  28.2 us (3%)
  between operations  14.3 us (2%)
    all_gather x1, waiting for transfers between devices, shards(): lax.all_gather(output_weight, 'dp', axis=0, tiled=True)  295 us
    all_gather x1, waiting for transfers between devices, shards(): lax.all_gather(query_weight, 'dp', axis=0, tiled=True)  187 us
    all_gather x1, waiting for transfers between devices, shards(): lax.all_gather(adapter_down_factors, 'dp', axis=0, tiled=True)  56.1 us
    all_gather x1, waiting for transfers between devices, shards(): lax.all_gather(key_value_weight, 'dp', axis=0, tiled=True)  54.8 us
    all_gather x1, waiting for transfers between devices, shards(): lax.all_gather(adapter_up_factors, 'dp', axis=0, tiled=True)  44.9 us
    dot_general x2, matrix products, add_rows(): return jnp.dot(normed, piece, preferred_element_type=jnp.float32)  22.2 us
    unnamed x10, local copies, waits for them, and re-layouts  17.3 us
    dot_general x1, matrix products, shards(): jnp.dot(context_all, lax.all_gather(output_weight, 'dp', axis=0, tiled=Tr...  17.2 us
  transfers between devices with their start and end apart: 6, of which 6 were waited for; matrix products, arithmetic and copies ran while one was open for 16% of the time, Pallas kernels for 0%

commit v1 on v0

--- a/solution.py
+++ b/solution.py
@@ -4,9 +4,28 @@
 import jax.numpy as jnp
 from jax import lax
 from jax.sharding import PartitionSpec as P
+from jax.experimental.layout import Layout, with_layout_constraint
 
 HEAD_SIZE = 64
 PAGE = 128
+
+
+def pack_columns(part, shard_rows):
+    flat = part.reshape(-1)
+    width = -(-flat.shape[0] // shard_rows)
+    flat = jnp.pad(flat, (0, width * shard_rows - flat.shape[0]))
+    return flat.reshape(shard_rows, width)
+
+
+def unpack_columns(block, shape):
+    shard_count = block.shape[0]
+    size = math.prod(shape)
+    flat = block.reshape(shard_count, -1)[:, :size]
+    return flat.reshape((shard_count * shape[0],) + tuple(shape[1:]))
+
+
+def row_major(x):
+    return with_layout_constraint(x, Layout(major_to_minor=tuple(range(x.ndim))))
 
 
 def layer_norm(tokens, layer_norm_gain, layer_norm_bias):
@@ -121,8 +140,18 @@
     def add_rows(piece):
         return jnp.dot(normed, piece, preferred_element_type=jnp.float32)
 
-    query_base = add_rows(lax.all_gather(query_weight, "dp", axis=0, tiled=True))
-    kv_base = add_rows(lax.all_gather(key_value_weight, "dp", axis=0, tiled=True))
+    shard_rows = query_weight.shape[0]
+    packed_parts = (query_weight, key_value_weight, adapter_down_factors, adapter_up_factors)
+    packed_cols = [pack_columns(part, shard_rows) for part in packed_parts]
+    widths = [part.shape[1] for part in packed_cols]
+    gathered = lax.all_gather(jnp.concatenate(packed_cols, axis=1), "dp", axis=0, tiled=False)
+    offsets = [sum(widths[:i]) for i in range(len(widths))]
+    unpacked = [
+        unpack_columns(gathered[:, :, off : off + width], part.shape)
+        for off, width, part in zip(offsets, widths, packed_parts)
+    ]
+    query_base = add_rows(unpacked[0])
+    kv_base = add_rows(unpacked[1])
     adapters_flat = prompt_adapter.reshape(total_prompts)
     adapter_count = adapter_storage.shape[0]
     adapter_numbers = jnp.arange(adapter_count, dtype=jnp.int32)
@@ -130,10 +159,7 @@
         jnp.where(adapter_numbers[None, :] == adapters_flat[:, None], adapter_storage[None, :], 0),
         axis=1,
     )
-    pieces = (
-        lax.all_gather(adapter_down_factors, "dp", axis=0, tiled=True),
-        lax.all_gather(adapter_up_factors, "dp", axis=0, tiled=True),
-    )
+    pieces = (unpacked[2], unpacked[3])
     piece_rows = pieces[0].shape[0]
     matches = (storage_slots[:, None] == jnp.arange(piece_rows, dtype=jnp.int32)[None, :]).astype(
         jnp.bfloat16
@@ -174,7 +200,7 @@
     context_all = lax.all_gather(context, "mp", axis=1, tiled=True)
     projected = jnp.dot(
         context_all,
-        lax.all_gather(output_weight, "dp", axis=0, tiled=True),
+        row_major(lax.all_gather(output_weight, "dp", axis=0, tiled=True)),
         preferred_element_type=jnp.float32,
     )
     attn_proj = projected.astype(jnp.bfloat16)

time: 820 us -> 508 us (0.62)
  waiting for transfers between devices: 657 us -> 312 us
  local copies, waits for them, and re-layouts: 28.2 us -> 69.8 us
    all_gather x1, waiting for transfers between devices: 295 us -> 64.9 us  [shards(): lax.all_gather(output_weight, 'dp', axis=0, tiled=True)]
    all_gather x4 -> x1, waiting for transfers between devices: 343 us -> 233 us  [shards(): lax.all_gather(jnp.concatenate(packed_cols, axis=1), 'dp', axis=0, tiled=...]
    another operation x0 -> x4, local copies, waits for them, and re-layouts: none -> 32 us  [unpack_columns(): return flat.reshape((shard_count * shape[0],) + tuple(shape[1:]))]
    slice x0 -> x6, local copies, waits for them, and re-layouts: none -> 18.8 us  [the longest x4 18.8 us: shards(): gathered[:, :, off:off + width]]
    unnamed x10 -> x47, local copies, waits for them, and re-layouts: 17.3 us -> 4.3 us
  transfers between devices with their start and end apart: 6 -> 3, of which waited for: 6 -> 3; matrix products, arithmetic and copies ran while one was open for 16% -> 31% of each run, Pallas kernels for 0% -> 0%
where the time goes in v1:
time: 508 us
  waiting for transfers between devices  312 us (61%)
  matrix products  79.2 us (16%)
  local copies, waits for them, and re-layouts  69.8 us (14%)
  other arithmetic  29.3 us (6%)
  between operations  14.2 us (3%)
    all_gather x1, waiting for transfers between devices, shards(): lax.all_gather(jnp.concatenate(packed_cols, axis=1), 'dp', axis=0, tiled=...  233 us
    all_gather x1, waiting for transfers between devices, shards(): lax.all_gather(output_weight, 'dp', axis=0, tiled=True)  64.9 us
    another operation x4, local copies, waits for them, and re-layouts, unpack_columns(): return flat.reshape((shard_count * shape[0],) + tuple(shape[1:]))  32 us
    dot_general x2, matrix products, add_rows(): return jnp.dot(normed, piece, preferred_element_type=jnp.float32)  20 us
    slice x4, local copies, waits for them, and re-layouts, shards(): gathered[:, :, off:off + width]  18.8 us
    dot_general x1, matrix products, shards(): jnp.dot(context_all, row_major(lax.all_gather(output_weight, 'dp', axis=0...  15.9 us
    dot_general x1, matrix products, attend(): jnp.einsum('hts,sd->thd', probs, values, preferred_element_type=jnp.float32)  14.6 us
    dot_general x1, matrix products, attend(): jnp.einsum('thd,sd->hts', queries, keys_rot, preferred_element_type=jnp.f...  14.3 us
  transfers between devices with their start and end apart: 3, of which 3 were waited for; matrix products, arithmetic and copies ran while one was open for 31% of the time, Pallas kernels for 0%

profile of v1, /device:TPU:0, one launch (start us, length us, event | category | flops | bytes accessed | tf_op | source)
XLA Modules:
  0.0 507.7 jit_solution(15966702300380031851)
XLA Ops:
  7.2 0.0 all-gather.10.cloned.1.call-start
  7.2 1.3 copy.44
  8.5 0.4 reshape.845
  8.9 0.0 copy-start.8
  8.9 0.0 copy-start.9
  9.0 0.9 copy.64
  9.8 0.3 reshape.847
  10.2 2.5 maximum_bitcast_fusion
  12.7 0.0 all-gather.10.cloned.1.call-update
  12.7 0.0 all-gather.8.cloned.1.call-start
  12.8 1.5 copy.51
  14.3 0.0 all-gather.8.cloned.1.call-update
  14.4 0.0 all-gather.6.cloned.1.call-start
  14.4 0.2 reduce_window_sum.11
  14.6 0.0 copy-start.2
  14.7 0.8 select_reduce_fusion.5
  15.5 0.1 select_reduce_fusion
  15.6 0.5 copy-done.15
  16.1 2.8 convert_reduce_fusion
  18.9 1.2 fusion.6
  20.1 0.6 fusion.103
  20.7 1.0 multiply_cosine_fusion
  21.7 0.9 fusion.48
  22.6 4.2 fusion.9
  26.8 233.2 %all-gather.10.cloned.1.call-done = bf16[16,284,2420]{2,1,0:T(8,128)(2,1)} async-done(((bf16[1,284,2420]{2,1,0:T(8,128)(2,1)}), bf16[16,284,2420]{2,1,0:T(8,128)(2,1)}) %all-gather.10.cloned.1.call-update) | async-done | bytes 21992976 | tf_op jit(solution)/shard_map/all_gather | solution.py:147
  260.0 1.8 fusion.100
  261.7 8.0 %reshape_reshape.11 = bf16[16,2272,16]{2,1,0:T(8,128)(2,1)} reshape(bf16[16,284,128]{2,1,0:T(8,128)(2,1)S(1)} %get-tuple-element.7) | data formatting | bytes 2326528 | tf_op jit(solution)/shard_map/reshape;reshape | solution.py:24
  269.7 7.8 %copy.47 = bf16[16,2272,16]{1,0,2:T(8,128)(2,1)S(1)} copy(bf16[16,2272,16]{2,1,0:T(8,128)(2,1)} %reshape_reshape.11) | data formatting | bytes 2326528 | tf_op jit(solution)/shard_map/reshape;reshape | solution.py:24
  277.5 2.7 reshape.849
  280.2 17.0 %slice.106 = bf16[16,284,2048]{2,1,0:T(8,128)(2,1)} slice(bf16[16,284,2420]{2,1,0:T(8,128)(2,1)} %all-gather.10.cloned.1.call-done), slice={[0:16], [0:284], [0:2048]} | slice | bytes 37224448 | tf_op jit(solution)/shard_map/slice | solution.py:150
  297.3 16.0 %reshape_reshape.10 = bf16[4544,2048]{1,0:T(8,128)(2,1)} reshape(bf16[16,284,2048]{2,1,0:T(8,128)(2,1)} %slice.106) | data formatting | bytes 37224448 | tf_op jit(solution)/shard_map/reshape;reshape | solution.py:24
  313.2 0.4 convolution_convert_fusion.1
  313.6 0.4 fusion.101
  314.1 2.9 fusion.37
  317.0 0.9 fusion.40
  317.9 0.9 fusion.43
  318.8 0.9 fusion.34
  319.8 3.6 psum.7
  323.4 0.4 convolution_convert_fusion.2
  323.7 0.4 fusion.102
  324.1 0.7 fusion.68
  324.8 2.4 fusion.71
  327.2 2.5 fusion.74
  329.8 2.5 fusion.65
  332.2 16.4 %add_add_fusion = f32[448,2048]{1,0:T(8,128)} fusion(f32[448,2048]{1,0:T(8,128)} %fusion.65, f32[448,2048]{1,0:T(8,128)S(1)} %fusion.68, f32[448,2048]{1,0:T(8,128)} %fusion.71, f32[448,2048]{1,0:T(8,128)} %fusion.74, bf16[448,4544]{1,0:T(8,128)(2,1)S(1)} %copy-done.1, bf16[4544,2048]{1,0:T(8,128)(2,1)} %reshape_reshape.10, f32[448]{0:T(512)S(1)} %bitcast.112, ...), kind=kOutput, calls=%fused_computation.17 | convolution fusion | flops 8345616384 | bytes 41040896 | tf_op jit(solution)/shard_map/dot_general | solution.py:141
  348.6 5.1 %copy.49 = f32[448,2048]{0,1:T(8,128)} copy(f32[448,2048]{1,0:T(8,128)} %add_add_fusion) | data formatting | bytes 7340032 | tf_op jit(solution)/shard_map/add | solution.py:187
  353.7 0.2 reshape_reshape.9
  354.0 3.6 fusion.104
  357.7 0.3 fusion.62
  358.1 0.7 subtract_convert_fusion
  358.8 14.3 %fusion.1 = (f32[32,448]{1,0:T(8,128)S(1)}, f32[448,448,32]{1,0,2:T(8,128)}) fusion(pred[448,448]{0,1:T(8,128)(4,1)S(1)} %copy-done.5, bf16[448,32,32]{0,2,1:T(8,128)(2,1)S(1)} %get-tuple-element.9, bf16[448,32,32]{0,2,1:T(8,128)(2,1)S(1)} %get-tuple-element.8, bf16[448,1,32]{0,2,1:T(8,128)(2,1)S(1)} %get-tuple-element.19, ...), kind=kOutput, calls=%fused_computation.5 | convolution fusion | flops 845121536 | bytes 27840512 | tf_op jit(solution)/shard_map/vmap(thd,sd->hts)/dot_general | solution.py:78
  373.0 13.2 %fusion = f32[32,448]{1,0:T(8,128)S(1)} fusion(f32[448,448,32]{1,0,2:T(8,128)} %get-tuple-element.29, f32[32,448]{1,0:T(8,128)S(1)} %get-tuple-element.28, pred[448,448]{0,1:T(8,128)(4,1)S(1)} %copy-done.5), kind=kLoop, calls=%fused_computation.4 | loop fusion | flops 25675776 | bytes 26005504 | tf_op jit(solution)/shard_map/vmap()/reduce_sum | solution.py:84
  386.3 14.6 %fusion.14 = bf16[64,32,448]{2,0,1:T(8,128)(2,1)} fusion(f32[32,448]{1,0:T(8,128)S(1)} %fusion, f32[32,448]{1,0:T(8,128)S(1)} %get-tuple-element.28, f32[448,448,32]{1,0,2:T(8,128)} %get-tuple-element.29, pred[448,448]{0,1:T(8,128)(4,1)S(1)} %copy-done.5, f32[448,128]{0,1:T(8,128)S(1)} %fusion.104), kind=kOutput, calls=%fused_computation.26 | convolution fusion | flops 855113728 | bytes 27951104 | tf_op jit(solution)/shard_map/vmap(hts,sd->thd)/dot_general | solution.py:85
  400.9 0.0 all-gather.6.cloned.1.call-update
  400.9 0.1 select_reduce_fusion.2
  401.1 0.1 select_reduce_fusion.4
  401.2 0.1 compare_select_fusion
  401.3 0.1 add_compare_fusion
  401.4 0.1 copy.52
  401.5 4.5 gather_fusion
  406.1 0.9 broadcast_select_fusion
  407.0 64.9 %all-gather.8.cloned.1.call-done = bf16[4096,2272]{1,0:T(8,128)(2,1)} async-done(((bf16[256,2272]{1,0:T(8,128)(2,1)}), bf16[4096,2272]{1,0:T(8,128)(2,1)}) %all-gather.8.cloned.1.call-update) | async-done | bytes 18612240 | tf_op jit(solution)/shard_map/all_gather | solution.py:203
  471.9 13.4 %all-gather.6.cloned.1.call-done = bf16[448,4096]{0,1:T(8,128)(2,1)} async-done(((bf16[448,2048]{0,1:T(8,128)(2,1)}), bf16[448,4096]{0,1:T(8,128)(2,1)}) %all-gather.6.cloned.1.call-update) | async-done | bytes 3670032 | tf_op jit(solution)/shard_map/all_gather | solution.py:200
  485.3 15.9 %convolution_convert_fusion = bf16[448,2272]{1,0:T(8,128)(2,1)} fusion(bf16[448,4096]{0,1:T(8,128)(2,1)} %all-gather.6.cloned.1.call-done, bf16[4096,2272]{1,0:T(8,128)(2,1)} %all-gather.8.cloned.1.call-done), kind=kOutput, calls=%fused_computation.16 | convolution fusion | flops 8339294208 | bytes 24317952 | tf_op jit(solution)/shard_map/dot_general | solution.py:201
  (60 shorter events, 0.2 us)
Async XLA Ops:
  7.2 5.6 %copy-start.4 = (bf16[256,2272]{0,1:T(8,128)(2,1)S(1)}, bf16[256,2272]{0,1:T(8,128)(2,1)}, u32[]{:S(2)}) copy-start(bf16[256,2272]{0,1:T(8,128)(2,1)} %param.17) | copy-start | bytes 3489796
  7.2 252.8 %all-gather.10.cloned.1.call-start = ((), (), s32[]{:S(2)}) async-start(), calls=%async_computation.2 | async-start | bytes 23814144 | tf_op jit(solution)/shard_map/all_gather | solution.py:147
  8.9 5.5 %copy-start.17 = (s32[1,4]{1,0:T(1,128)S(1)}, s32[1,4]{1,0:T(1,128)}, u32[]{:S(2)}) copy-start(s32[1,4]{1,0:T(1,128)} %param.20) | copy-start | bytes 52
  8.9 5.7 %copy-start.8 = (bf16[4544]{0:T(1024)(128)(2,1)S(1)}, bf16[4544]{0:T(1024)(128)(2,1)}, u32[]{:S(2)}) copy-start(bf16[4544]{0:T(1024)(128)(2,1)} %param.13) | copy-start | bytes 27268
  8.9 5.7 %copy-start.9 = (bf16[4544]{0:T(1024)(128)(2,1)S(1)}, bf16[4544]{0:T(1024)(128)(2,1)}, u32[]{:S(2)}) copy-start(bf16[4544]{0:T(1024)(128)(2,1)} %param.14) | copy-start | bytes 27268
  8.9 5.7 %copy-start.19 = (s32[16]{0:T(128)S(1)}, s32[16]{0:T(128)}, u32[]{:S(2)}) copy-start(s32[16]{0:T(128)} %param.23) | copy-start | bytes 196
  8.9 5.7 %copy-start.20 = (s32[1,4]{1,0:T(1,128)S(1)}, s32[1,4]{1,0:T(1,128)}, u32[]{:S(2)}) copy-start(s32[1,4]{1,0:T(1,128)} %param.21) | copy-start | bytes 52
  12.7 459.1 %all-gather.8.cloned.1.call-start = ((), (), s32[]{:S(2)}) async-start(), calls=%async_computation.1 | async-start | bytes 20054016 | tf_op jit(solution)/shard_map/all_gather | solution.py:203
  14.4 470.9 %all-gather.6.cloned.1.call-start = ((), (), s32[]{:S(2)}) async-start(), calls=%async_computation | async-start | bytes 6291456 | tf_op jit(solution)/shard_map/all_gather | solution.py:200
  14.6 4.2 copy-start.2
  14.7 6.1 %copy-start.11 = (f32[32]{0:T(128)}, f32[32]{0:T(128)S(1)}, u32[]{:S(2)}) copy-start(f32[32]{0:T(128)S(1)} %multiply_exponential_fusion) | copy-start | bytes 388
  15.5 0.6 copy-start.15
  269.7 7.8 %slice-start = ((bf16[16,284,2420]{2,1,0:T(8,128)(2,1)}), bf16[16,284,116]{2,1,0:T(8,128)(2,1)S(1)}, s32[]{:S(2)}) async-start(bf16[16,284,2420]{2,1,0:T(8,128)(2,1)} %all-gather.10.cloned.1.call-done), calls=%async_computation.3 | async-start | bytes 2359296 | tf_op jit(solution)/shard_map/slice | solution.py:150
  297.3 16.0 %copy-start.13 = (s32[4]{0:T(128)S(1)}, s32[4]{0:T(128)}, u32[]{:S(2)}) copy-start(s32[4]{0:T(128)} %select_reduce_fusion.5) | copy-start | bytes 52
  313.2 3.8 copy-start
  314.0 9.3 %slice-start.1 = ((bf16[16,32944]{1,0:T(8,128)(2,1)}), bf16[16,32768]{1,0:T(8,128)(2,1)S(1)}, s32[]{:S(2)}) async-start(bf16[16,32944]{1,0:T(8,128)(2,1)} %reshape.849), calls=%async_computation.4 | async-start | bytes 2097152 | tf_op jit(solution)/shard_map/slice | solution.py:23
  314.1 9.3 %copy-start.14 = (s32[4]{0:T(128)S(1)}, s32[4]{0:T(128)}, u32[]{:S(2)}) copy-start(s32[4]{0:T(128)} %select_reduce_fusion.5) | copy-start | bytes 52
  327.2 5.0 copy-start.1
  327.2 5.0 copy-start.10
  354.0 3.7 copy-start.12
  354.0 4.0 copy-start.3
  354.0 4.0 copy-start.6
  354.0 4.0 copy-start.7
  357.7 1.1 copy-start.5
  386.3 14.7 %copy-start.21 = (s32[1,8]{1,0:T(1,128)S(1)}, s32[1,8]{1,0:T(1,128)}, u32[]{:S(2)}) copy-start(s32[1,8]{1,0:T(1,128)} %param.22) | copy-start | bytes 100
  386.3 14.8 %copy-start.16 = (s32[4]{0:T(128)S(1)}, s32[4]{0:T(128)}, u32[]{:S(2)}) copy-start(s32[4]{0:T(128)} %copy-done.15) | copy-start | bytes 52
  386.3 14.8 %copy-start.18 = (s32[1,4]{1,0:T(1,128)S(1)}, s32[1,4]{1,0:T(1,128)}, u32[]{:S(2)}) copy-start(s32[1,4]{1,0:T(1,128)} %param.20) | copy-start | bytes 52
Sparse Core Ops, SparseCore 0:
  12.9 247.0 all-gather.9
  262.7 209.0 all-gather.7
  473.4 11.8 all-gather.5

commit v2 on v1

--- a/solution.py
+++ b/solution.py
@@ -1,9 +1,10 @@
+import functools
 import math
 
 import jax
 import jax.numpy as jnp
 from jax import lax
-from jax.sharding import PartitionSpec as P
+from jax.sharding import Mesh, PartitionSpec as P
 from jax.experimental.layout import Layout, with_layout_constraint
 
 HEAD_SIZE = 64
@@ -104,6 +105,28 @@
     valid = within < prompt_len[:, None]
     source = jnp.minimum(base_row[:, None] + within, kv_rot.shape[0] - 1)
     return jnp.where(valid[:, :, None], kv_rot[source], jnp.zeros((), kv_rot.dtype))
+
+
+def swap(x, axis_name):
+    return lax.ppermute(x, axis_name, [(0, 1), (1, 0)])
+
+
+def in_order(own, other, first):
+    lower = jnp.where(first, own, other)
+    upper = jnp.where(first, other, own)
+    return lower, upper
+
+
+def mp_gather(x, axis, mp_count):
+    if mp_count == 2:
+        lower, upper = in_order(x, swap(x, "mp"), lax.axis_index("mp") == 0)
+        return jnp.concatenate([lower, upper], axis=axis)
+    return lax.all_gather(x, "mp", axis=axis, tiled=True)
+
+
+def half_of(x, axis, which):
+    width = x.shape[axis] // 2
+    return lax.dynamic_slice_in_dim(x, which * width, width, axis)
 
 
 def shards(
@@ -119,118 +142,185 @@
     prompt_adapter,
     prompt_page_table,
     adapter_storage,
+    mp_count,
 ):
-    row_number_count = tokens.shape[0]
+    side = lax.axis_index("dl")
+    first = side == 0
+    mp_index = lax.axis_index("mp")
+    own_rows = tokens.shape[0]
     group_count = lengths.shape[0]
-    group_rows = row_number_count // group_count
+    group_rows = own_rows // group_count
     prompt_count = lengths.shape[1]
-    total_prompts = group_count * prompt_count
-    member_grouped, position_grouped, start_grouped, index_grouped = jax.vmap(
-        lambda one_row: layout(one_row, group_rows)
-    )(lengths)
-    position = position_grouped.reshape(row_number_count)
-    prompt_global = (
-        index_grouped + (jnp.arange(group_count, dtype=jnp.int32) * prompt_count)[:, None]
-    ).reshape(row_number_count)
-    member_weight = (
-        prompt_global[:, None] == jnp.arange(total_prompts, dtype=jnp.int32)[None, :]
-    ).astype(jnp.float32)
+    pair_rows = 2 * own_rows
+
     normed = layer_norm(tokens, layer_norm_gain, layer_norm_bias)
 
-    def add_rows(piece):
-        return jnp.dot(normed, piece, preferred_element_type=jnp.float32)
-
     shard_rows = query_weight.shape[0]
-    packed_parts = (query_weight, key_value_weight, adapter_down_factors, adapter_up_factors)
-    packed_cols = [pack_columns(part, shard_rows) for part in packed_parts]
-    widths = [part.shape[1] for part in packed_cols]
-    gathered = lax.all_gather(jnp.concatenate(packed_cols, axis=1), "dp", axis=0, tiled=False)
+    rank_width = adapter_down_factors.shape[2]
+    kept = (
+        half_of(query_weight, 1, side),
+        key_value_weight,
+        adapter_down_factors,
+        half_of(adapter_up_factors, 2, side),
+    )
+    sent = (
+        half_of(query_weight, 1, 1 - side),
+        key_value_weight,
+        adapter_down_factors,
+        half_of(adapter_up_factors, 2, 1 - side),
+    )
+    kept_cols = [pack_columns(part, shard_rows) for part in kept]
+    widths = [part.shape[1] for part in kept_cols]
+    kept_block = jnp.concatenate(kept_cols, axis=1)
+    sent_block = jnp.concatenate([pack_columns(part, shard_rows) for part in sent], axis=1)
+    lower, upper = in_order(kept_block, swap(sent_block, "dl"), first)
+    gathered = lax.all_gather(jnp.stack([lower, upper]), "dh", axis=0, tiled=False)
+    gathered = gathered.reshape((-1,) + gathered.shape[2:])
     offsets = [sum(widths[:i]) for i in range(len(widths))]
     unpacked = [
         unpack_columns(gathered[:, :, off : off + width], part.shape)
-        for off, width, part in zip(offsets, widths, packed_parts)
+        for off, width, part in zip(offsets, widths, kept)
     ]
-    query_base = add_rows(unpacked[0])
-    kv_base = add_rows(unpacked[1])
-    adapters_flat = prompt_adapter.reshape(total_prompts)
+    query_cols, kv_weight, down_all, up_cols = unpacked
+
+    out_kept = half_of(output_weight, 1, side)
+    out_sent = half_of(output_weight, 1, 1 - side)
+    lower, upper = in_order(out_kept, swap(out_sent, "dl"), first)
+    out_gathered = lax.all_gather(jnp.stack([lower, upper]), "dh", axis=0, tiled=False)
+    out_cols = row_major(out_gathered.reshape(-1, out_kept.shape[1]))
+
+    row_half = own_rows // mp_count
+    partner_piece = swap(lax.dynamic_slice_in_dim(normed, mp_index * row_half, row_half, 0), "dl")
+    partner_normed = mp_gather(partner_piece, 0, mp_count)
+    lower, upper = in_order(normed, partner_normed, first)
+    normed_pair = jnp.concatenate([lower, upper], axis=0)
+    small = jnp.concatenate([lengths, prompt_adapter], axis=1)
+    lower, upper = in_order(small, swap(small, "dl"), first)
+    small_pair = jnp.concatenate([lower, upper], axis=0)
+    lengths_pair = small_pair[:, :prompt_count]
+    adapter_pair = small_pair[:, prompt_count:]
+
+    member_grouped, position_grouped, start_grouped, index_grouped = jax.vmap(
+        lambda one_row: layout(one_row, group_rows)
+    )(lengths_pair)
+    pair_groups = 2 * group_count
+    pair_prompts = pair_groups * prompt_count
+    position = position_grouped.reshape(pair_rows)
+    prompt_global = (
+        index_grouped + (jnp.arange(pair_groups, dtype=jnp.int32) * prompt_count)[:, None]
+    ).reshape(pair_rows)
+    member = prompt_global[:, None] == jnp.arange(pair_prompts, dtype=jnp.int32)[None, :]
+
     adapter_count = adapter_storage.shape[0]
     adapter_numbers = jnp.arange(adapter_count, dtype=jnp.int32)
+    adapters_flat = adapter_pair.reshape(pair_prompts)
     storage_slots = jnp.sum(
         jnp.where(adapter_numbers[None, :] == adapters_flat[:, None], adapter_storage[None, :], 0),
         axis=1,
     )
-    pieces = (unpacked[2], unpacked[3])
-    piece_rows = pieces[0].shape[0]
-    matches = (storage_slots[:, None] == jnp.arange(piece_rows, dtype=jnp.int32)[None, :]).astype(
+    slot_rows = down_all.shape[0]
+    matches = (storage_slots[:, None] == jnp.arange(slot_rows, dtype=jnp.int32)[None, :]).astype(
         jnp.bfloat16
     )
-    down_part = jnp.einsum("pn,ndr->pdr", matches, pieces[0], preferred_element_type=jnp.float32)
-    up_part = jnp.einsum("pn,nrc->prc", matches, pieces[1], preferred_element_type=jnp.float32)
-    down_selected = down_part.astype(jnp.bfloat16)
-    up_selected = up_part.astype(jnp.bfloat16)
+    down_selected = jnp.einsum(
+        "pn,ndr->pdr", matches, down_all, preferred_element_type=jnp.float32
+    ).astype(jnp.bfloat16)
+    up_selected = jnp.einsum(
+        "pn,nrc->prc", matches, up_cols, preferred_element_type=jnp.float32
+    ).astype(jnp.bfloat16)
+
     feature_columns = adapter_down_factors.shape[1]
-    features = lax.dynamic_slice_in_dim(
-        normed, lax.axis_index("mp") * feature_columns, feature_columns, 1
-    )
-    rank_portion = jnp.zeros((row_number_count, adapter_down_factors.shape[2]), jnp.float32)
-    for prompt in range(total_prompts):
-        rank_portion = rank_portion + member_weight[:, prompt : prompt + 1] * jnp.dot(
-            features, down_selected[prompt], preferred_element_type=jnp.float32
-        )
+    features = lax.dynamic_slice_in_dim(normed, mp_index * feature_columns, feature_columns, 1)
+    own_prompts = group_count * prompt_count
+    own_down = lax.dynamic_slice_in_dim(down_selected, (1 - first.astype(jnp.int32)) * own_prompts, own_prompts, 0)
+    own_member = lax.dynamic_slice_in_dim(member, (1 - first.astype(jnp.int32)) * own_rows, own_rows, 0)
+    own_member = lax.dynamic_slice_in_dim(own_member, (1 - first.astype(jnp.int32)) * own_prompts, own_prompts, 1)
+    all_ranks = jnp.dot(
+        features,
+        jnp.transpose(own_down, (1, 0, 2)).reshape(feature_columns, own_prompts * rank_width),
+        preferred_element_type=jnp.float32,
+    ).reshape(own_rows, own_prompts, rank_width)
+    rank_portion = jnp.sum(jnp.where(own_member[:, :, None], all_ranks, 0.0), axis=1)
     ranks = lax.psum(rank_portion, "mp").astype(jnp.bfloat16)
-    adapted_queries = jnp.zeros((row_number_count, adapter_up_factors.shape[2]), jnp.float32)
-    for prompt in range(total_prompts):
-        adapted_queries = adapted_queries + member_weight[:, prompt : prompt + 1] * jnp.dot(
-            ranks, up_selected[prompt], preferred_element_type=jnp.float32
-        )
+    lower, upper = in_order(ranks, swap(ranks, "dl"), first)
+    ranks_pair = jnp.concatenate([lower, upper], axis=0)
+    spread = jnp.where(member[:, :, None], ranks_pair[:, None, :], jnp.zeros((), jnp.bfloat16))
+    adapted_queries = jnp.dot(
+        spread.reshape(pair_rows, pair_prompts * rank_width),
+        up_selected.reshape(pair_prompts * rank_width, -1),
+        preferred_element_type=jnp.float32,
+    )
+
+    query_base = jnp.dot(normed_pair, query_cols, preferred_element_type=jnp.float32)
+    kv_base = jnp.dot(normed_pair, kv_weight, preferred_element_type=jnp.float32)
     queries = rotate(
-        (query_base + adapted_queries).reshape(row_number_count, -1, HEAD_SIZE), position
+        (query_base + adapted_queries).reshape(pair_rows, -1, HEAD_SIZE), position
     ).astype(jnp.bfloat16)
     keys_rot = rotate(kv_base[:, None, :HEAD_SIZE], position)[:, 0, :]
     kv_rot = jnp.concatenate([keys_rot, kv_base[:, HEAD_SIZE:]], axis=1).astype(jnp.bfloat16)
     local_heads = queries.shape[1]
-    queries_grouped = queries.reshape(group_count, group_rows, local_heads, HEAD_SIZE)
-    kv_grouped = kv_rot.reshape(group_count, group_rows, 2 * HEAD_SIZE)
+    queries_grouped = queries.reshape(pair_groups, group_rows, local_heads, HEAD_SIZE)
+    kv_grouped = kv_rot.reshape(pair_groups, group_rows, 2 * HEAD_SIZE)
     context_grouped = jax.vmap(
         lambda q_part, kv_part, idx_part: attend(
             q_part, kv_part[:, :HEAD_SIZE], kv_part[:, HEAD_SIZE:], idx_part
         )
     )(queries_grouped, kv_grouped, index_grouped)
-    context = context_grouped.reshape(row_number_count, local_heads * HEAD_SIZE)
-    context_all = lax.all_gather(context, "mp", axis=1, tiled=True)
-    projected = jnp.dot(
-        context_all,
-        row_major(lax.all_gather(output_weight, "dp", axis=0, tiled=True)),
+    context = context_grouped.reshape(pair_rows, local_heads * HEAD_SIZE)
+
+    lower, upper = in_order(context, swap(context, "dl"), first)
+    context_all = mp_gather(jnp.concatenate([lower, upper], axis=1), 1, mp_count)
+    own_start = (1 - first.astype(jnp.int32)) * own_rows
+    partner_start = first.astype(jnp.int32) * own_rows
+    partner_out = jnp.dot(
+        lax.dynamic_slice_in_dim(context_all, partner_start, own_rows, 0),
+        out_cols,
         preferred_element_type=jnp.float32,
-    )
-    attn_proj = projected.astype(jnp.bfloat16)
+    ).astype(jnp.bfloat16)
+    received_out = swap(partner_out, "dl")
+    own_out = jnp.dot(
+        lax.dynamic_slice_in_dim(context_all, own_start, own_rows, 0),
+        out_cols,
+        preferred_element_type=jnp.float32,
+    ).astype(jnp.bfloat16)
+    lower, upper = in_order(own_out, received_out, first)
+    attn_proj = jnp.concatenate([lower, upper], axis=1)
+
+    own_groups = lax.dynamic_slice_in_dim(kv_grouped, (1 - first.astype(jnp.int32)) * group_count, group_count, 0)
+    own_starts = lax.dynamic_slice_in_dim(start_grouped, (1 - first.astype(jnp.int32)) * group_count, group_count, 0)
     cache_grouped = jax.vmap(
         lambda kv_part, len_part, start_part, table_part: fill_pages(
             kv_part, len_part, start_part, table_part, PAGE
         )
-    )(kv_grouped, lengths, start_grouped, prompt_page_table)
+    )(own_groups, lengths, own_starts, prompt_page_table)
     kv_cache = cache_grouped.reshape(group_count * prompt_page_table.shape[1], PAGE, 2 * HEAD_SIZE)
     return (attn_proj, kv_cache)
 
 
 def solution(mesh):
+    dp_count = mesh.shape["dp"]
+    mp_count = mesh.shape["mp"]
+    pair_mesh = Mesh(
+        mesh.devices.reshape(dp_count // 2, 2, mp_count), ("dh", "dl", "mp")
+    )
+    dp = ("dh", "dl")
     return jax.shard_map(
-        shards,
-        mesh=mesh,
+        functools.partial(shards, mp_count=mp_count),
+        mesh=pair_mesh,
         in_specs=(
-            P("dp", None),
+            P(dp, None),
             P(),
             P(),
-            P("dp", "mp"),
-            P("dp", None),
-            P("dp", "mp"),
-            P("dp", "mp", None),
-            P("dp", None, "mp"),
-            P("dp", None),
-            P("dp", None),
-            P("dp", None),
+            P(dp, "mp"),
+            P(dp, None),
+            P(dp, "mp"),
+            P(dp, "mp", None),
+            P(dp, None, "mp"),
+            P(dp, None),
+            P(dp, None),
+            P(dp, None),
             P(),
         ),
-        out_specs=(P("dp", "mp"), P("dp", None, None)),
+        out_specs=(P(dp, "mp"), P(dp, None, None)),
         check_vma=False,
     )

time: 508 us -> 465 us (0.915); the launches traced: 508 us -> 457 us
  waiting for transfers between devices: 312 us -> 226 us
  local copies, waits for them, and re-layouts: 69.8 us -> 87.8 us
  other arithmetic: 29.3 us -> 45.7 us
  starting transfers between devices: 0.12 us -> 9.35 us
  matrix products: 79.2 us -> 70.2 us
    all_gather x3 -> x2, waiting for transfers between devices: 311 us -> 98.2 us  [shards(): lax.all_gather(jnp.stack([lower, upper]), 'dh', axis=0, tiled=False)]
    ppermute x0 -> x9, waiting for transfers between devices: none -> 128 us  [swap(): return lax.ppermute(x, axis_name, [(0, 1), (1, 0)])]
    dot_general x14 -> x8, matrix products: 64.6 us -> 40.5 us  [the longest x1 12.8 us: shards(): jnp.dot(normed_pair, query_cols, preferred_element_type=jnp.float32)]
    select_n x0 -> x6, other arithmetic: none -> 21.8 us  [the longest x5 13 us: in_order(): lower = jnp.where(first, own, other)]
    sub x0 -> x1, matrix products: none -> 16.3 us  [attend(): weights = jnp.exp(scores - row_peak)]
    reduce_sum x1 -> x0, other arithmetic: 13.2 us -> none  [attend(): jnp.sum(weights, axis=-1, keepdims=True)]
    all_gather x0 -> x1, local copies, waits for them, and re-layouts: none -> 12.8 us  [shards(): lax.all_gather(jnp.stack([lower, upper]), 'dh', axis=0, tiled=False)]
    ppermute x0 -> x9, starting transfers between devices: none -> 9.27 us  [swap(): return lax.ppermute(x, axis_name, [(0, 1), (1, 0)])]
  transfers between devices with their start and end apart: 3 -> 11, of which waited for: 3 -> 6; matrix products, arithmetic and copies ran while one was open for 31% -> 35% of each run, Pallas kernels for 0% -> 0%
where the time goes in v2:
time: 465 us; the launch traced here: 457 us
  waiting for transfers between devices  226 us (49%)
  local copies, waits for them, and re-layouts  87.8 us (19%)
  matrix products  70.2 us (15%)
  other arithmetic  45.7 us (10%)
  between operations  14.6 us (3%)
  starting transfers between devices  9.35 us (2%)
    ppermute x9, waiting for transfers between devices, swap(): return lax.ppermute(x, axis_name, [(0, 1), (1, 0)])  128 us
    all_gather x2, waiting for transfers between devices, shards(): lax.all_gather(jnp.stack([lower, upper]), 'dh', axis=0, tiled=False)  98.2 us
    another operation x4, local copies, waits for them, and re-layouts, unpack_columns(): return flat.reshape((shard_count * shape[0],) + tuple(shape[1:]))  26 us
    sub x1, matrix products, attend(): weights = jnp.exp(scores - row_peak)  16.3 us
    dot_general x1, matrix products, attend(): jnp.einsum('hts,sd->thd', probs, values, preferred_element_type=jnp.float32)  13.4 us
    select_n x5, other arithmetic, in_order(): lower = jnp.where(first, own, other)  13 us
    all_gather x1, local copies, waits for them, and re-layouts, shards(): lax.all_gather(jnp.stack([lower, upper]), 'dh', axis=0, tiled=False)  12.8 us
    dot_general x1, matrix products, shards(): jnp.dot(normed_pair, query_cols, preferred_element_type=jnp.float32)  12.8 us
  transfers between devices with their start and end apart: 11, of which 6 were waited for; matrix products, arithmetic and copies ran while one was open for 35% of the time, Pallas kernels for 0%

profile of v2, /device:TPU:0, one launch (start us, length us, event | category | flops | bytes accessed | tf_op | source)
XLA Modules:
  0.0 457.0 jit_solution(10014285447413544151)
XLA Ops:
  7.2 1.3 constant_dynamic-slice_fusion.3
  8.6 0.8 dynamic-slice_bitcast_fusion.1
  9.6 1.2 copy.62
  11.2 1.0 fusion.39
  12.1 3.0 collective-permute-start.2
  15.4 17.8 %collective-permute-done.2 = bf16[284,1338]{1,0:T(8,128)(2,1)S(1)} collective-permute-done((bf16[284,1338]{1,0:T(8,128)(2,1)S(1)}, bf16[284,1338]{1,0:T(8,128)(2,1)S(1)}, u32[]{:S(2)}, u32[]{:S(2)}) %collective-permute-start.2) | collective-permute-done | bytes 760016 | tf_op jit(solution)/shard_map/ppermute | solution.py:111
  33.6 1.4 pad_maximum_fusion.9
  35.1 3.0 convert_reduce_fusion
  38.1 0.4 copy-done
  38.5 1.2 fusion.8
  39.8 2.3 fusion.11
  42.0 2.0 copy-done.5
  44.1 1.4 constant_dynamic-slice_fusion.4
  45.5 1.7 collective-permute-start
  47.6 0.9 constant_dynamic-slice_fusion.1
  48.5 1.7 collective-permute-start.7
  50.3 43.3 %collective-permute-done.3 = s32[1,8]{1,0:T(1,128)S(1)} collective-permute-done((s32[1,8]{1,0:T(1,128)S(1)}, s32[1,8]{1,0:T(1,128)S(1)}, u32[]{:S(2)}, u32[]{:S(2)}) %collective-permute-start.3) | collective-permute-done | bytes 64 | tf_op jit(solution)/shard_map/ppermute | solution.py:111
  94.2 0.6 eq.128
  95.0 0.9 select_reduce_fusion.3
  95.9 1.2 multiply_cosine_fusion
  97.0 1.2 compare_and_fusion
  98.2 6.2 %collective-permute-done.7 = bf16[256,1136]{0,1:T(8,128)(2,1)} collective-permute-done((bf16[256,1136]{0,1:T(8,128)(2,1)}, bf16[256,1136]{0,1:T(8,128)(2,1)}, u32[]{:S(2)}, u32[]{:S(2)}) %collective-permute-start.7) | collective-permute-done | bytes 581664 | tf_op jit(solution)/shard_map/ppermute | solution.py:111
  104.4 1.3 select_bitcast_fusion.3
  105.7 1.1 pad_maximum_fusion.16
  106.9 2.6 broadcast_select_fusion.5
  109.5 1.4 copy-done.1
  110.9 8.5 %broadcast_select_fusion.1 = (bf16[448,4544]{1,0:T(8,128)(2,1)}, bf16[448,4544]{1,0:T(8,128)(2,1)}) fusion(pred[]{:T(512)S(6)} %eq.119, bf16[224,4544]{1,0:T(8,128)(2,1)S(1)} %get-tuple-element.13, bf16[224,4544]{1,0:T(8,128)(2,1)S(1)} %get-tuple-element.12, f32[4544]{0:T(1024)S(1)} %convert_element_type.65, f32[4544]{0:T(1024)S(1)} %convert_element_type.64, ...), kind=kLoop, calls=%fused_computation.31 | loop fusion | flops 24428544 | bytes 16325633 | tf_op jit(solution)/shard_map/jit(_where)/select_n | solution.py:115
  119.3 98.2 %all-gather.5.cloned.1.call-done = bf16[16,284,1338]{2,1,0:T(8,128)(2,1)} async-done(((bf16[2,284,1338]{2,1,0:T(8,128)(2,1)}), bf16[16,284,1338]{2,1,0:T(8,128)(2,1)}) %all-gather.5.cloned.1.call-update) | async-done | bytes 12159760 | tf_op jit(solution)/shard_map/all_gather | solution.py:177
  217.6 1.8 fusion.92
  219.6 8.0 %reshape_reshape.11 = bf16[16,2272,16]{2,1,0:T(8,128)(2,1)} reshape(bf16[16,284,128]{2,1,0:T(8,128)(2,1)S(1)} %get-tuple-element.7) | data formatting | bytes 2326528 | tf_op jit(solution)/shard_map/reshape;reshape | solution.py:25
  227.6 7.8 %copy.63 = bf16[16,2272,16]{1,0,2:T(8,128)(2,1)S(1)} copy(bf16[16,2272,16]{2,1,0:T(8,128)(2,1)} %reshape_reshape.11) | data formatting | bytes 2326528 | tf_op jit(solution)/shard_map/reshape;reshape | solution.py:25
  235.9 2.6 fusion.35
  238.6 3.4 psum.7
  242.0 1.6 collective-permute-start.4
  243.6 1.8 reshape.646
  245.4 5.2 %fusion.13 = f32[896,128]{0,1:T(8,128)S(1)} fusion(bf16[4544,128]{1,0:T(8,128)(2,1)S(1)} %reshape_reshape.9, bf16[448,4544]{1,0:T(8,128)(2,1)} %get-tuple-element.9, bf16[448,4544]{1,0:T(8,128)(2,1)} %get-tuple-element.8), kind=kOutput, calls=%fused_computation.24 | convolution fusion | flops 1058570240 | bytes 9764864 | tf_op jit(solution)/shard_map/dot_general | solution.py:255
  250.6 0.5 fusion.59
  251.8 8.9 %slice.62 = bf16[16,284,1024]{2,1,0:T(8,128)(2,1)} slice(bf16[16,284,1338]{2,1,0:T(8,128)(2,1)} %all-gather.5.cloned.1.call-done), slice={[0:16], [0:284], [0:1024]} | slice | bytes 18612224 | tf_op jit(solution)/shard_map/slice | solution.py:181
  260.7 10.0 %reshape_reshape.10 = bf16[4544,1024]{1,0:T(8,128)(2,1)} reshape(bf16[16,284,1024]{2,1,0:T(8,128)(2,1)} %slice.62) | data formatting | bytes 18612224 | tf_op jit(solution)/shard_map/reshape;reshape | solution.py:25
  270.8 0.7 fusion.45
  271.5 3.9 copy-done.4
  275.4 12.8 %bitcast_add_fusion = f32[896,1024]{1,0:T(8,128)} fusion(f32[896,1024,1]{1,0,2:T(8,128)S(1)} %fusion.45, bf16[4544,1024]{1,0:T(8,128)(2,1)S(1)} %copy-done.4, bf16[448,4544]{1,0:T(8,128)(2,1)} %get-tuple-element.9, bf16[448,4544]{1,0:T(8,128)(2,1)} %get-tuple-element.8), kind=kOutput, calls=%fused_computation.33 | convolution fusion | flops 8355479552 | bytes 24788992 | tf_op jit(solution)/shard_map/dot_general | solution.py:254
  288.2 5.1 %copy.67 = f32[896,1024]{0,1:T(8,128)} copy(f32[896,1024]{1,0:T(8,128)} %bitcast_add_fusion) | data formatting | bytes 7340032 | tf_op jit(solution)/shard_map/add | solution.py:257
  293.3 2.6 subtract_convert_fusion
  295.9 0.9 concatenate.62
  297.0 0.9 concatenate.63
  297.8 1.2 copy.69
  299.0 16.3 %fusion.94 = (f32[2,16,448]{2,1,0:T(8,128)S(1)}, f32[2,16,448,448]{2,3,1,0:T(8,128)}) fusion(pred[2,448,448]{1,2,0:T(8,128)(4,1)} %compare_and_fusion, bf16[2,448,16,32]{1,3,2,0:T(8,128)(2,1)} %copy.69, bf16[2,448,16,32]{1,3,2,0:T(8,128)(2,1)S(1)} %copy.68, bf16[2,448,64,1]{1,0,2,3:T(2,128)(2,1)S(1)} %bitcast.89), kind=kOutput, calls=%fused_computation.174 | convolution fusion | flops 851444160 | bytes 28098560 | tf_op jit(solution)/shard_map/vmap()/sub | solution.py:84
  315.3 13.4 %convert_bitcast_fusion = bf16[2,448,16,64]{1,3,2,0:T(8,128)(2,1)} fusion(f32[2,16,448,448]{2,3,1,0:T(8,128)} %get-tuple-element.41, f32[2,16,448]{2,1,0:T(8,128)S(1)} %get-tuple-element.40, bf16[2,448,64,1]{1,0,2,3:T(2,128)(2,1)S(1)} %bitcast.90), kind=kOutput, calls=%fused_computation.40 | convolution fusion | flops 835846144 | bytes 27697152 | tf_op jit(solution)/shard_map/vmap(hts,sd->thd)/dot_general | solution.py:86
  328.7 3.8 copy.73
  332.4 2.6 reshape.649
  335.2 41.9 %collective-permute-done.5 = bf16[896,1024]{0,1:T(8,128)(2,1)S(1)} collective-permute-done((bf16[896,1024]{0,1:T(8,128)(2,1)}, bf16[896,1024]{0,1:T(8,128)(2,1)S(1)}, u32[]{:S(2)}, u32[]{:S(2)}) %collective-permute-start.5) | collective-permute-done | bytes 1835040 | tf_op jit(solution)/shard_map/ppermute | solution.py:111
  377.1 1.8 broadcast_select_fusion.7
  379.0 1.2 copy-done.2
  380.2 2.2 pad_maximum_fusion.4
  382.6 12.8 %copy.74 = bf16[16,256,1136]{2,1,0:T(8,128)(2,1)} copy(bf16[16,256,1136]{1,2,0:T(8,128)(2,1)} %all-gather.7.cloned.1.call-done) | data formatting | bytes 18612224 | tf_op jit(solution)/shard_map/all_gather | solution.py:189
  395.4 8.8 %broadcast_select_fusion.2 = (bf16[896,2048]{0,1:T(8,128)(2,1)}, bf16[896,2048]{0,1:T(8,128)(2,1)}) fusion(bf16[896,2048]{0,1:T(8,128)(2,1)} %collective-permute-done.6, pred[]{:T(512)S(6)} %eq.120, bf16[896,1024]{0,1:T(8,128)(2,1)} %copy-done.2, bf16[896,1024]{0,1:T(8,128)(2,1)S(1)} %get-tuple-element.16), kind=kLoop, calls=%fused_computation.34 | loop fusion | flops 11010048 | bytes 14680065 | tf_op jit(solution)/shard_map/jit(_where)/select_n | solution.py:116
  404.2 7.9 %fusion.23 = bf16[448,1136]{1,0:T(8,128)(2,1)S(1)} fusion(bf16[4096,1136]{1,0:T(8,128)(2,1)S(1)} %bitcast.86, s32[]{:T(128)S(6)} %mul.198, bf16[896,2048]{0,1:T(8,128)(2,1)} %get-tuple-element.11, bf16[896,2048]{0,1:T(8,128)(2,1)} %get-tuple-element.10), kind=kOutput, calls=%fused_computation.37 | convolution fusion | flops 4176987136 | bytes 17664004 | tf_op jit(solution)/shard_map/dot_general | solution.py:275
  412.1 0.7 collective-permute-start.8
  413.4 4.7 %gather_fusion = bf16[1024,128]{1,0:T(8,128)(2,1)S(1)} fusion(bf16[1,448,128]{2,1,0:T(8,128)(2,1)S(1)} %fusion.62, s32[1024]{0:T(1024)S(1)} %fusion.68), kind=kCustom, calls=%fused_computation | custom fusion | bytes 532480 | tf_op jit(solution)/shard_map/vmap()/gather | solution.py:107
  418.1 0.9 broadcast_select_fusion.10
  419.0 18.3 %collective-permute-done.8 = bf16[448,1136]{1,0:T(8,128)(2,1)S(1)} collective-permute-done((bf16[448,1136]{1,0:T(8,128)(2,1)S(1)}, bf16[448,1136]{1,0:T(8,128)(2,1)S(1)}, u32[]{:S(2)}, u32[]{:S(2)}) %collective-permute-start.8) | collective-permute-done | bytes 1017888 | tf_op jit(solution)/shard_map/ppermute | solution.py:111
  437.4 10.8 %broadcast_select_fusion.9 = (bf16[448,1136]{1,0:T(8,128)(2,1)S(1)}, bf16[448,1136]{1,0:T(8,128)(2,1)S(1)}) fusion(bf16[448,1136]{1,0:T(8,128)(2,1)S(1)} %collective-permute-done.8, pred[]{:T(512)S(6)} %eq.119, bf16[4096,1136]{1,0:T(8,128)(2,1)} %bitcast.85, s32[]{:T(128)S(6)} %select_n.269, bf16[896,2048]{0,1:T(8,128)(2,1)} %get-tuple-element.11, ...), kind=kOutput, calls=%fused_computation.63 | convolution fusion | flops 4178004992 | bytes 19699716 | tf_op jit(solution)/shard_map/dot_general | solution.py:281
  448.1 1.8 pad_maximum_fusion.6
  (90 shorter events, 5.5 us)
Async XLA Ops:
  7.2 26.1 %copy-start.9 = (bf16[284,128]{1,0:T(8,128)(2,1)S(1)}, bf16[284,128]{1,0:T(8,128)(2,1)}, u32[]{:S(2)}) copy-start(bf16[284,128]{1,0:T(8,128)(2,1)} %param.16) | copy-start | bytes 218116
  7.2 210.4 %all-gather.5.cloned.1.call-start = ((), (), s32[]{:S(2)}) async-start(), calls=%async_computation | async-start | bytes 14598144 | tf_op jit(solution)/shard_map/all_gather | solution.py:177
  12.1 21.1 %collective-permute-start.2 = (bf16[284,1338]{1,0:T(8,128)(2,1)S(1)}, bf16[284,1338]{1,0:T(8,128)(2,1)S(1)}, u32[]{:S(2)}, u32[]{:S(2)}) collective-permute-start(bf16[284,1338]{1,0:T(8,128)(2,1)S(1)} %fusion.39), channel_id=1, source_target_pairs={{0,2},{2,0},{1,3},{3,1},{4,6},{6,4},{5,7},{7,5},{8,10},{10,8},{9,1... | collective-permute-start | bytes 2279960 | tf_op jit(solution)/shard_map/ppermute | solution.py:111
  15.2 19.9 %copy-start.10 = (bf16[4544]{0:T(1024)(128)(2,1)S(1)}, bf16[4544]{0:T(1024)(128)(2,1)}, u32[]{:S(2)}) copy-start(bf16[4544]{0:T(1024)(128)(2,1)} %param.13) | copy-start | bytes 27268
  15.2 19.9 %copy-start.11 = (bf16[4544]{0:T(1024)(128)(2,1)S(1)}, bf16[4544]{0:T(1024)(128)(2,1)}, u32[]{:S(2)}) copy-start(bf16[4544]{0:T(1024)(128)(2,1)} %param.14) | copy-start | bytes 27268
  35.0 347.6 %all-gather.7.cloned.1.call-start = ((), (), s32[]{:S(2)}) async-start(), calls=%async_computation.1 | async-start | bytes 10469376 | tf_op jit(solution)/shard_map/all_gather | solution.py:189
  35.1 3.4 copy-start
  42.0 2.1 copy-start.5
  44.1 3.2 copy-start.12
  44.1 3.2 copy-start.13
  44.1 3.5 copy-start.6
  45.5 48.4 %collective-permute-start = (bf16[224,4544]{1,0:T(8,128)(2,1)}, bf16[224,4544]{1,0:T(8,128)(2,1)S(1)}, u32[]{:S(2)}, u32[]{:S(2)}) collective-permute-start(bf16[224,4544]{1,0:T(8,128)(2,1)} %constant_dynamic-slice_fusion.4), channel_id=1, source_target_pairs={{0,2},{2,0},{1,3},{3,1},{4,6},{6,4},{5,7},{7,5},{8,10},{10,8},{9,1... | collective-permute-start | bytes 6107144 | tf_op jit(solution)/shard_map/ppermute | solution.py:111
  47.4 46.3 %collective-permute-start.3 = (s32[1,8]{1,0:T(1,128)S(1)}, s32[1,8]{1,0:T(1,128)S(1)}, u32[]{:S(2)}, u32[]{:S(2)}) collective-permute-start(s32[1,8]{1,0:T(1,128)S(1)} %pad_add_fusion.1), channel_id=1, source_target_pairs={{0,2},{2,0},{1,3},{3,1},{4,6},{6,4},{5,7},{7,5},{8,10},{10,8},{9,1... | collective-permute-start | bytes 104 | tf_op jit(solution)/shard_map/ppermute | solution.py:111
  48.5 55.9 %collective-permute-start.7 = (bf16[256,1136]{0,1:T(8,128)(2,1)}, bf16[256,1136]{0,1:T(8,128)(2,1)}, u32[]{:S(2)}, u32[]{:S(2)}) collective-permute-start(bf16[256,1136]{0,1:T(8,128)(2,1)} %constant_dynamic-slice_fusion.1), channel_id=1, source_target_pairs={{0,2},{2,0},{1,3},{3,1},{4,6},{6,4},{5,7},{7,5},{8,10},{10,8},{9,1... | collective-permute-start | bytes 1744904 | tf_op jit(solution)/shard_map/ppermute | solution.py:111
  93.9 12.9 %collective-permute-start.1 = (bf16[224,4544]{1,0:T(8,128)(2,1)S(1)}, bf16[224,4544]{1,0:T(8,128)(2,1)}, u32[]{:S(2)}, u32[]{:S(2)}) collective-permute-start(bf16[224,4544]{1,0:T(8,128)(2,1)S(1)} %collective-permute-done), channel_id=1, source_target_pairs={{0,1},{1,0},{2,3},{3,2},{4,5},{5,4},{6,7},{7,6},{8,9},{9,8},{10,11... | collective-permute-start | bytes 6107144 | tf_op jit(solution)/shard_map/ppermute | solution.py:111
  106.8 4.0 copy-start.1
  235.4 8.2 %slice-start = ((bf16[16,284,1338]{2,1,0:T(8,128)(2,1)}), bf16[16,284,58]{2,1,0:T(8,128)(2,1)S(1)}, s32[]{:S(2)}) async-start(bf16[16,284,1338]{2,1,0:T(8,128)(2,1)} %all-gather.5.cloned.1.call-done), calls=%async_computation.2 | async-start | bytes 2359296 | tf_op jit(solution)/shard_map/slice | solution.py:181
  242.0 28.7 %collective-permute-start.4 = (bf16[448,16]{0,1:T(8,128)(2,1)S(1)}, bf16[448,16]{0,1:T(8,128)(2,1)S(1)}, u32[]{:S(2)}, u32[]{:S(2)}) collective-permute-start(bf16[448,16]{0,1:T(8,128)(2,1)S(1)} %psum.7), channel_id=1, source_target_pairs={{0,2},{2,0},{1,3},{3,1},{4,6},{6,4},{5,7},{7,5},{8,10},{10,8},{9,1... | collective-permute-start | bytes 43016 | tf_op jit(solution)/shard_map/ppermute | solution.py:111
  270.8 4.6 %copy-start.4 = (bf16[4544,1024]{1,0:T(8,128)(2,1)S(1)}, bf16[4544,1024]{1,0:T(8,128)(2,1)}, u32[]{:S(2)}) copy-start(bf16[4544,1024]{1,0:T(8,128)(2,1)} %reshape_reshape.10) | copy-start | bytes 27918340
  288.2 5.1 %copy-start.7 = (f32[896,32]{0,1:T(8,128)S(1)}, f32[896,32]{0,1:T(8,128)}, u32[]{:S(2)}) copy-start(f32[896,32]{0,1:T(8,128)} %get-tuple-element.32) | copy-start | bytes 344068
  288.2 5.1 %copy-start.8 = (f32[896,32]{0,1:T(8,128)S(1)}, f32[896,32]{0,1:T(8,128)}, u32[]{:S(2)}) copy-start(f32[896,32]{0,1:T(8,128)} %get-tuple-element.33) | copy-start | bytes 344068
  335.0 42.1 %collective-permute-start.5 = (bf16[896,1024]{0,1:T(8,128)(2,1)}, bf16[896,1024]{0,1:T(8,128)(2,1)S(1)}, u32[]{:S(2)}, u32[]{:S(2)}) collective-permute-start(bf16[896,1024]{0,1:T(8,128)(2,1)} %reshape.649), channel_id=1, source_target_pairs={{0,2},{2,0},{1,3},{3,1},{4,6},{6,4},{5,7},{7,5},{8,10},{10,8},{9,1... | collective-permute-start | bytes 5505032 | tf_op jit(solution)/shard_map/ppermute | solution.py:111
  379.0 1.2 copy-start.2
  379.0 3.4 copy-start.14
  382.4 13.0 %collective-permute-start.6 = (bf16[896,2048]{0,1:T(8,128)(2,1)}, bf16[896,2048]{0,1:T(8,128)(2,1)}, u32[]{:S(2)}, u32[]{:S(2)}) collective-permute-start(bf16[896,2048]{0,1:T(8,128)(2,1)} %pad_maximum_fusion.4), channel_id=1, source_target_pairs={{0,1},{1,0},{2,3},{3,2},{4,5},{5,4},{6,7},{7,6},{8,9},{9,8},{10,11... | collective-permute-start | bytes 11010056 | tf_op jit(solution)/shard_map/ppermute | solution.py:111
  395.4 8.8 %copy-start.3 = (bf16[16,256,1136]{2,1,0:T(8,128)(2,1)S(1)}, bf16[16,256,1136]{2,1,0:T(8,128)(2,1)}, u32[]{:S(2)}) copy-start(bf16[16,256,1136]{2,1,0:T(8,128)(2,1)} %copy.74) | copy-start | bytes 27918340
  412.1 25.3 %collective-permute-start.8 = (bf16[448,1136]{1,0:T(8,128)(2,1)S(1)}, bf16[448,1136]{1,0:T(8,128)(2,1)S(1)}, u32[]{:S(2)}, u32[]{:S(2)}) collective-permute-start(bf16[448,1136]{1,0:T(8,128)(2,1)S(1)} %fusion.23), channel_id=1, source_target_pairs={{0,2},{2,0},{1,3},{3,1},{4,6},{6,4},{5,7},{7,5},{8,10},{10,8},{9,1... | collective-permute-start | bytes 3053576 | tf_op jit(solution)/shard_map/ppermute | solution.py:111
Sparse Core Ops, SparseCore 0:
  35.1 182.3 all-gather.4
  219.7 133.8 all-gather.6
